TPU v7x, 512 devices: a whole 4x4x16 slice. The times are simulated.
512 devices in a mesh: dp: 32 (over z, core), seq: 16 (over y, x).
Axes of the slice: x: 4, y: 4, z: 16, core: 2. Of those that a mesh axis runs over, the one named last changes fastest.
Arguments:
- mixer_in: bfloat16 [131072, 2816], P(('dp', 'seq')), parts along dimension 0, may hold values from -92 to 92
- gate_input: bfloat16 [131072, 2560], P(('dp', 'seq')), parts along dimension 0, may hold values from -6 to 6
- step_raw: bfloat16 [131072, 40], P(('dp', 'seq')), parts along dimension 0, may hold values from -6 to 6
- lengths: int32 [96], P('dp'), parts along dimension 0, may hold values from 1 to 2048, 4096 in all
- deal_order: int32 [512], P('dp'), parts along dimension 0, may hold values from 0 to 15, as said below
- conv_weight: float32 [4, 2816], replicated, may hold values from -3 to 3
- conv_bias: float32 [2816], replicated, may hold values from -3 to 3
- step_bias: float32 [40], replicated, may hold values from -4 to -1
- decay_rate: float32 [40], replicated, may hold values from 0.01 to 2
- skip_gain: float32 [40], replicated, may hold values from 0.5 to 1.5
- norm_gain: float32 [2560], replicated, may hold values from 0.5 to 1.5
Outputs:
- mixed_out: bfloat16 [131072, 2560], P(('dp', 'seq')), parts along dimension 0
- final_states: float32 [96, 2560, 128], P('dp', 'seq'), parts along dimension 0
There are 32 independent parts, one for each index of `dp`. A program takes and returns all parts, laid end to end along the dimension named above; an argument that names none is the same for every part. Nothing has to cross between parts.
Inputs may be any that keep to these rules, and one draw needn't show every extreme that they name: The prompt lengths sum to 4096 and the longest is exactly 2048. `deal_order`: every sequence stretch stands in exactly one dealt slot.
All inputs are finite; a program needn't handle non-finite values.
Results may differ from a plain program's by a relative error of at most 0.005.
Values may be sent and summed in bfloat16 or wider, within the bound.
No kernel may reach another device: no remote copies, remote signals or barrier semaphores. Data moves between devices by JAX's collectives and lax.ppermute only.
A program may use at most 128 MiB of HBM per device.

v0:
```python
import jax
import jax.numpy as jnp
from jax import lax
from jax.sharding import PartitionSpec as P

HEADS = 40
HEAD_DIM = 64
STATE = 128
KERNEL = 4
STRETCH = 256
DOCS = 3
INNER = 2560
CHANNELS = 2816


def doc_index(ends, positions):
    return jnp.sum((ends[None, :] <= positions[:, None]).astype(jnp.int32), axis=1)


def body(
    mixer_in,
    gate_input,
    step_raw,
    lengths,
    deal_order,
    conv_weight,
    conv_bias,
    step_bias,
    decay_rate,
    skip_gain,
    norm_gain,
):
    myself = lax.axis_index("seq")
    local_rows = mixer_in.shape[0]
    stretches_here = local_rows // STRETCH
    stretch_total = deal_order.shape[0]
    ends = jnp.cumsum(lengths)
    all_stretches = jnp.arange(stretch_total, dtype=jnp.int32)
    my_stretches = lax.dynamic_slice_in_dim(deal_order, myself * stretches_here, stretches_here)
    lane = jnp.arange(STRETCH, dtype=jnp.int32)
    own_doc = doc_index(
        ends, (my_stretches[:, None] * STRETCH + lane[None, :]).reshape(-1)
    ).reshape(stretches_here, STRETCH)
    prev_own = jnp.where(my_stretches > 0, doc_index(ends, my_stretches * STRETCH - 1), -1)
    blocks_in = mixer_in.reshape(stretches_here, STRETCH, CHANNELS)
    tails = blocks_in[:, STRETCH - (KERNEL - 1) :, :]
    step_blocks = step_raw.reshape(stretches_here, STRETCH, HEADS)
    step = jax.nn.softplus(step_blocks.astype(jnp.float32) + step_bias)
    log_decay = -decay_rate * step
    all_tails, all_steps = (
        lax.all_gather(tails, "seq", axis=0, tiled=True),
        lax.all_gather(step_blocks, "seq", axis=0, tiled=True),
    )
    totals = jnp.sum(
        -decay_rate * jax.nn.softplus(all_steps.astype(jnp.float32) + step_bias), axis=1
    )
    slot_map = (deal_order[:, None] == all_stretches[None, :]).astype(jnp.float32)
    packed_totals = jnp.dot(slot_map.T, totals, precision=lax.Precision.HIGHEST)
    prefix = jnp.cumsum(packed_totals, axis=0)
    base = jnp.concatenate([jnp.zeros((1, HEADS), jnp.float32), prefix[:-1]], 0)
    pick_own = (my_stretches[:, None] == all_stretches[None, :]).astype(jnp.float32)
    base_own = jnp.dot(pick_own, base, precision=lax.Precision.HIGHEST)
    running = base_own[:, None, :] + jnp.cumsum(log_decay, axis=1)
    prev_pick = (deal_order[None, :] == my_stretches[:, None] - 1).astype(jnp.bfloat16)
    prev_rows = jnp.einsum(
        "is,skc->ikc", prev_pick, all_tails, preferred_element_type=jnp.float32
    ).astype(jnp.bfloat16)
    extended = jnp.concatenate([prev_rows, blocks_in], 1)
    lead = (
        my_stretches[:, None] * STRETCH
        - (KERNEL - 1)
        + jnp.arange(KERNEL - 1, dtype=jnp.int32)[None, :]
    ).reshape(-1)
    ext_doc = jnp.concatenate(
        [doc_index(ends, lead).reshape(stretches_here, KERNEL - 1), own_doc], 1
    )
    accum = jnp.zeros((stretches_here, STRETCH, CHANNELS), jnp.float32) + conv_bias
    for offset in range(KERNEL):
        keep = (ext_doc[:, offset : offset + STRETCH] == own_doc).astype(jnp.float32)
        accum = (
            accum
            + conv_weight[offset]
            * extended[:, offset : offset + STRETCH, :].astype(jnp.float32)
            * keep[..., None]
        )
    mixed = jax.nn.silu(accum).astype(jnp.bfloat16)
    values = mixed[..., :INNER]
    input_map = mixed[..., INNER : INNER + STATE]
    output_map = mixed[..., INNER + STATE :]
    scaled = (values.astype(jnp.float32) * jnp.repeat(step, HEAD_DIM, axis=2)).astype(jnp.bfloat16)
    end_weight = jnp.exp(
        jnp.where((own_doc == own_doc[:, -1:])[..., None], running[:, -1:, :] - running, -jnp.inf)
    )
    weighted = (scaled.astype(jnp.float32) * jnp.repeat(end_weight, HEAD_DIM, axis=2)).astype(
        jnp.bfloat16
    )
    states = jnp.einsum("isk,isn->ikn", weighted, input_map, preferred_element_type=jnp.float32)
    source_pick = (deal_order[:, None] == all_stretches[None, :]).astype(jnp.float32)
    source_end = jnp.dot(source_pick, prefix, precision=lax.Precision.HIGHEST)
    source_doc = doc_index(ends, deal_order * STRETCH + STRETCH - 1)
    allowed = (deal_order[None, :] < my_stretches[:, None]) & (
        source_doc[None, :] == prev_own[:, None]
    )
    spans = jnp.exp(
        jnp.where(allowed[..., None], base_own[:, None, :] - source_end[None, :, :], -jnp.inf)
    )
    state_in = jnp.einsum(
        "ick,ckn->ikn",
        jnp.repeat(spans, HEAD_DIM, axis=2),
        lax.all_gather(states, "seq", axis=0, tiled=True),
        precision=lax.Precision.HIGHEST,
    )
    later = lane[:, None] >= lane[None, :]
    direct_gain = jnp.repeat(skip_gain, HEAD_DIM)[None, :]

    def stretch_out(inputs):
        values_c, scaled_c, keys_c, queries_c, running_c, doc_c, base_c, prev_c, state_c = inputs
        scores = jnp.dot(queries_c, keys_c.T, preferred_element_type=jnp.float32)
        same = (doc_c[:, None] == doc_c[None, :]) & later
        spans = running_c.T[:, :, None] - running_c.T[:, None, :]
        mixing = (scores[None] * jnp.exp(jnp.where(same[None], spans, -jnp.inf))).astype(
            jnp.bfloat16
        )
        within = jnp.einsum(
            "hts,shp->thp",
            mixing,
            scaled_c.reshape(STRETCH, HEADS, HEAD_DIM),
            preferred_element_type=jnp.float32,
        ).reshape(STRETCH, INNER)
        readout = jnp.dot(
            queries_c, state_c.astype(jnp.bfloat16).T, preferred_element_type=jnp.float32
        )
        carry_weight = jnp.exp(
            jnp.where((doc_c == prev_c)[:, None], running_c - base_c[None, :], -jnp.inf)
        )
        return (
            within
            + readout * jnp.repeat(carry_weight, HEAD_DIM, axis=1)
            + values_c.astype(jnp.float32) * direct_gain
        )

    outputs = lax.map(
        stretch_out,
        (values, scaled, input_map, output_map, running, own_doc, base_own, prev_own, state_in),
    )
    gated = outputs.reshape(local_rows, INNER) * jax.nn.silu(gate_input.astype(jnp.float32))
    normed = gated * lax.rsqrt(jnp.mean(gated * gated, axis=1, keepdims=True) + 1e-05) * norm_gain
    mixed_out = normed.astype(jnp.bfloat16)
    slot_numbers = jnp.arange(stretches_here, dtype=jnp.int32)

    def one_doc(document):
        last = lax.dynamic_index_in_dim(ends, document, keepdims=False) - 1
        owner = last // STRETCH
        match = my_stretches == owner
        slot = jnp.sum(jnp.where(match, slot_numbers, 0))

        def present():
            within_pos = last - owner * STRETCH
            running_c = lax.dynamic_index_in_dim(running, slot, keepdims=False)
            running_e = lax.dynamic_index_in_dim(running_c, within_pos, keepdims=False)
            doc_c = lax.dynamic_index_in_dim(own_doc, slot, keepdims=False)
            scaled_c = lax.dynamic_index_in_dim(scaled, slot, keepdims=False)
            keys_c = lax.dynamic_index_in_dim(input_map, slot, keepdims=False)
            base_c = lax.dynamic_index_in_dim(base_own, slot, keepdims=False)
            prev_c = lax.dynamic_index_in_dim(prev_own, slot, keepdims=False)
            state_c = lax.dynamic_index_in_dim(state_in, slot, keepdims=False)
            weight = jnp.exp(
                jnp.where((doc_c == document)[:, None], running_e[None, :] - running_c, -jnp.inf)
            )
            final_weighted = (
                scaled_c.astype(jnp.float32) * jnp.repeat(weight, HEAD_DIM, axis=1)
            ).astype(jnp.bfloat16)
            part = jnp.dot(final_weighted.T, keys_c, preferred_element_type=jnp.float32)
            carry_weight = jnp.exp(jnp.where(prev_c == document, running_e - base_c, -jnp.inf))
            return part + jnp.repeat(carry_weight, HEAD_DIM)[:, None] * state_c

        def absent():
            return jnp.zeros((INNER, STATE), jnp.float32)

        return lax.cond(jnp.any(match), present, absent)

    every_doc = jnp.transpose(lax.map(one_doc, jnp.arange(DOCS, dtype=jnp.int32)), (1, 0, 2))
    kept = lax.psum_scatter(
        every_doc.astype(jnp.bfloat16), "seq", scatter_dimension=0, tiled=True
    ).astype(jnp.float32)
    final_states = jnp.transpose(kept, (1, 0, 2))
    return (mixed_out, final_states)


def solution(mesh):
    return jax.shard_map(
        body,
        mesh=mesh,
        in_specs=(
            P(("dp", "seq"), None),
            P(("dp", "seq"), None),
            P(("dp", "seq"), None),
            P("dp"),
            P("dp"),
            P(),
            P(),
            P(),
            P(),
            P(),
            P(),
        ),
        out_specs=(P(("dp", "seq"), None), P("dp", "seq", None)),
        check_vma=False,
    )
```

profile of v0, /device:TPU:2, one launch (start us, length us, event | category | flops | bytes accessed | tf_op | source)
XLA Modules:
  0.0 391.7 jit_solution(15185379277083827339)
XLA Ops:
  7.2 0.7 neg.23
  7.9 26.9 %all-gather = bf16[4096,40]{0,1:T(8,128)(2,1)S(1)} all-gather(bf16[256,40]{0,1:T(8,128)(2,1)} %param.17), channel_id=2, replica_groups=mesh['dp'=32,'seq'=16] {'seq'}, dimensions={0}, use_global_device_ids=true | all-gather | bytes 348160 | tf_op jit(solution)/shard_map/all_gather | solution.py:52
  34.8 0.8 multiply_bitcast_fusion
  35.7 0.6 reduce-window.11
  36.5 1.2 dynamic_slice.62
  39.0 0.8 reduce-window.10
  40.1 0.6 slice.90
  40.8 0.8 slice.76
  41.6 21.6 %all_gather.9 = bf16[16,3,2816]{2,1,0:T(4,128)(2,1)S(1)} all-gather(bf16[1,3,2816]{2,1,0:T(4,128)(2,1)S(1)} %slice.76), channel_id=1, replica_groups=mesh['dp'=32,'seq'=16] {'seq'}, dimensions={0}, use_global_device_ids=true | all-gather | bytes 287232 | tf_op jit(solution)/shard_map/all_gather | solution.py:51
  63.2 0.8 fusion.32
  64.1 1.1 slice_reduce_fusion.5
  65.4 2.1 copy.73
  67.5 0.6 fusion.55
  69.0 0.6 fusion.30
  70.1 0.8 fusion.42
  71.1 0.6 slice_reduce_fusion.1
  72.3 0.6 broadcast_compare_fusion.1
  73.3 2.1 copy.78
  75.5 5.9 %multiply_convert_fusion.2 = bf16[1,256,2816]{2,1,0:T(8,128)(2,1)S(1)} fusion(bf16[256,2816]{1,0:T(8,128)(2,1)} %param.15, bf16[1,3,2816]{2,1,0:T(4,128)(2,1)S(1)} %copy.108, bf16[1,256,2816]{2,1,0:T(8,128)(2,1)} %bitcast.153, f32[2816]{0:T(1024)S(1)} %get-tuple-element.357, f32[256]{0:T(256)S(1)} %bitcast.173, f32[2816]{0:T(1024)S(1)} %get-tuple-element.358, ...), kind=kLoop, calls=%fused_computation.33 | loop fusion | flops 20905984 | bytes 4401664 | tf_op jit(solution)/shard_map/convert_element_type | solution.py:86
  81.8 1.9 copy-done.1
  83.7 1.8 fusion.25
  85.8 1.4 copy.74
  87.3 0.7 compare_and_fusion
  88.2 146.0 %all-gather.4.cloned.1.call-done = f32[40960,128]{1,0:T(8,128)} async-done(((f32[2560,128]{1,0:T(8,128)}), f32[40960,128]{1,0:T(8,128)}) %all-gather.4.cloned.1.call-update) | async-done | bytes 20971536 | tf_op jit(solution)/shard_map/all_gather | solution.py:110
  234.4 38.9 %fusion.6 = f32[2560,1,128]{2,1,0:T(1,128)S(1)} fusion(f32[16,2560,1]{0,2,1:T(1,128)S(1)} %bitcast.151, f32[16,2560,128]{2,1,0:T(8,128)} %bitcast.147), kind=kOutput, calls=%fused_computation.15 | convolution fusion | flops 62914560 | bytes 22446080 | tf_op jit(solution)/shard_map/ick,ckn->ikn/dot_general | solution.py:107
  273.3 20.2 %while.17 = (s32[]{:T(128)}, bf16[3,2560,128]{2,1,0:T(8,128)(2,1)}, s32[3]{0:T(128)S(1)}, s32[3]{0:T(128)S(1)}, s32[1]{0:T(128)}, /*index=5*/bf16[1,256,2560]{1,...) while((s32[]{:T(128)}, bf16[3,2560,128]{2,1,0:T(8,128)(2,1)}, ...), condition=%wide.region_13.14_spmd, body=%wide.region_10.13_spmd.sunk | while | flops 170742112 | bytes 7442075 | solution.py:182
  273.3 0.6 dynamic_slice.66
  275.8 0.6 dynamic_slice.67
  277.7 4.0 %conditional.2 = (bf16[1,2560,128]{2,1,0:T(8,128)(2,1)S(1)}) conditional(s32[]{:T(128)} %bitcast.143, () %tuple.66, (bf16[1,256,2560]{1,2,0:T(8,128)(2,1)}, s32[]{:T(128)}, s32[1,256]{1,0:T(1,128)S(1)}, s32[]{:T(128)}, s32[]{:T(128)}, /*index=5*/f32[1,256,40]{1,2,0:T(8,128)S(1)}, bf16[1,256,128]{2,1,0:T(8,128)(2,1)S(1)}, s32[1]{0:T(128)}, ...), branch_computations={%region_11.11_spmd, %region_12.12_spmd} | conditional | flops 170742096 | bytes 6130356 | solution.py:180
  277.9 0.7 compare_reduce_fusion
  278.6 1.7 fusion.1
  281.1 0.5 fusion
  281.7 0.9 constant_dynamic-update-slice_fusion.2
  282.5 0.6 dynamic_slice.66
  285.1 0.6 dynamic_slice.67
  287.1 0.9 constant_dynamic-update-slice_fusion.2
  288.0 0.6 dynamic_slice.66
  290.5 0.6 dynamic_slice.67
  292.5 0.9 constant_dynamic-update-slice_fusion.2
  293.5 1.1 fusion.36
  294.6 5.1 %fusion.8 = f32[40,64,256]{2,1,0:T(8,128)} fusion(bf16[256,40,64]{0,2,1:T(8,128)(2,1)} %bitcast.28, f32[40,256]{1,0:T(8,128)S(1)} %bitcast.154, f32[256,256]{1,0:T(8,128)S(1)} %fusion.36, pred[256,256]{1,0:T(8,128)(4,1)S(1)} %fusion.34), kind=kOutput, calls=%fused_computation.18 | convolution fusion | flops 346030080 | bytes 4300800 | tf_op jit(solution)/shard_map/while/body/eval_jaxpr/hts,shp->thp/dot_general | solution.py:124
  299.7 3.2 copy.80
  303.0 1.7 broadcast_in_dim.192
  304.7 3.4 copy.79
  308.2 4.6 %multiply_reduce_fusion = (f32[256]{0:T(256)S(1)}, f32[256,2560]{1,0:T(8,128)S(1)}) fusion(bf16[256,2560]{1,0:T(8,128)(2,1)S(1)} %copy-done.8, f32[2560]{0:T(1024)S(1)} %mul.239, bf16[1,256,2816]{2,1,0:T(8,128)(2,1)} %copy-done.2, f32[256,2560]{1,0:T(8,128)} %copy.80, f32[256,2560]{1,0:T(8,128)} %copy.79, f32[2560,128]{1,0:T(8,128)S(1)} %bitcast.146), kind=kOutput, calls=%fused_computation.40 | convolution fusion | flops 176619264 | bytes 11873280 | tf_op jit(solution)/shard_map/while/body/eval_jaxpr/dot_general | solution.py:130
  312.9 1.3 multiply_convert_fusion.3
  314.2 69.0 %reduce-scatter.2.cloned.1.call-done = bf16[160,3,128]{2,0,1:T(8,128)(2,1)} async-done(((bf16[2560,3,128]{2,0,1:T(8,128)(2,1)}), bf16[160,3,128]{2,0,1:T(8,128)(2,1)}) %reduce-scatter.2.cloned.1.call-update) | async-done | bytes 122896 | tf_op jit(solution)/shard_map/reduce_scatter | solution.py:183
  383.3 1.6 convert_bitcast_fusion.2
  (67 shorter events, 4.3 us)
Async XLA Ops:
  7.2 227.1 %all-gather.4.cloned.1.call-start = ((), (), s32[]{:S(2)}) async-start(), calls=%async_computation.2 | async-start | bytes 22282240 | tf_op jit(solution)/shard_map/all_gather | solution.py:110
  65.4 3.7 copy-start.6
  67.5 2.1 copy-start.5
  73.3 2.1 copy-start.4
  75.5 5.9 %copy-start = (f32[1,256,2560]{2,1,0:T(8,128)S(1)}, f32[1,256,2560]{2,1,0:T(8,128)}, u32[]{:S(2)}) copy-start(f32[1,256,2560]{2,1,0:T(8,128)} %copy.73) | copy-start | bytes 7864324
  81.4 153.0 %copy-start.2 = (bf16[1,256,2816]{2,1,0:T(8,128)(2,1)}, bf16[1,256,2816]{2,1,0:T(8,128)(2,1)S(1)}, u32[]{:S(2)}) copy-start(bf16[1,256,2816]{2,1,0:T(8,128)(2,1)S(1)} %multiply_convert_fusion.2) | copy-start | bytes 4325380
  81.4 2.3 copy-start.1
  85.5 297.7 %reduce-scatter.2.cloned.1.call-start = ((), (), s32[]{:S(2)}) async-start(), calls=%async_computation.1 | async-start | bytes 2088960 | tf_op jit(solution)/shard_map/reduce_scatter | solution.py:183
  304.7 3.4 copy-start.7
  304.7 3.5 copy-start.8
  308.2 4.7 %copy-start.3 = (f32[2560]{0:T(1024)S(1)}, f32[2560]{0:T(1024)}, u32[]{:S(2)}) copy-start(f32[2560]{0:T(1024)} %param.25) | copy-start | bytes 30724
Sparse Core Ops, SparseCore 0:
  85.7 148.5 all-gather.3
  293.6 89.6 reduce-scatter.1
where the time goes:
time: 393 us; the launch traced here: 392 us
  waiting for transfers between devices  215 us (55%)
  matrix products  54 us (14%)
  blocking collectives  48.5 us (12%)
  local copies, waits for them, and re-layouts  28.5 us (7%)
  other arithmetic  18 us (5%)
  between operations  17 us (4%)
  loops' own time  10.3 us (3%)
    all_gather x1, waiting for transfers between devices, body(): lax.all_gather(states, 'seq', axis=0, tiled=True)  146 us
    reduce_scatter x1, waiting for transfers between devices, body(): lax.psum_scatter(every_doc.astype(jnp.bfloat16), 'seq', scatter_dimension...  69 us
    dot_general x1, matrix products, body(): jnp.einsum('ick,ckn->ikn', jnp.repeat(spans, HEAD_DIM, axis=2), lax.all_g...  38.9 us
    all_gather x1, blocking collectives, body(): lax.all_gather(step_blocks, 'seq', axis=0, tiled=True)  26.9 us
    all_gather x1, blocking collectives, body(): lax.all_gather(tails, 'seq', axis=0, tiled=True)  21.6 us
    another operation x1, loops' own time, body(): lax.map(one_doc, jnp.arange(DOCS, dtype=jnp.int32))  9.57 us
  transfers between devices with their start and end apart: 2, of which 2 were waited for; matrix products, arithmetic and copies ran while one was open for 6% of the time, Pallas kernels for 0%

commit v1 on v0

--- a/solution.py
+++ b/solution.py
@@ -11,6 +11,19 @@
 DOCS = 3
 INNER = 2560
 CHANNELS = 2816
+
+
+def ring_gather(array, axis, dim):
+    ways = lax.axis_size(axis)
+    up = [(d, (d + 1) % ways) for d in range(ways)]
+    down = [(d, (d - 1) % ways) for d in range(ways)]
+    earlier, later = ([array], [array])
+    for _ in range(ways // 2):
+        earlier.append(lax.ppermute(earlier[-1], axis, up))
+    for _ in range((ways - 1) // 2):
+        later.append(lax.ppermute(later[-1], axis, down))
+    line = jnp.concatenate([*earlier[::-1], *later[1:]], axis=dim)
+    return jnp.roll(line, (lax.axis_index(axis) - ways // 2) * array.shape[dim], axis=dim)
 
 
 def doc_index(ends, positions):
@@ -49,7 +62,7 @@
     log_decay = -decay_rate * step
     all_tails, all_steps = (
         lax.all_gather(tails, "seq", axis=0, tiled=True),
-        lax.all_gather(step_blocks, "seq", axis=0, tiled=True),
+        ring_gather(step_blocks, "seq", 0),
     )
     totals = jnp.sum(
         -decay_rate * jax.nn.softplus(all_steps.astype(jnp.float32) + step_bias), axis=1

time: 393 us -> 443 us (1.13)
  starting transfers between devices: 0.26 us -> 63.7 us
  blocking collectives: 48.5 us -> 26.3 us
    ppermute x0 -> x15, starting transfers between devices: none -> 63.4 us  [the longest x7 41.9 us: ring_gather(): later.append(lax.ppermute(later[-1], axis, down))]
    all_gather x1 -> x0, blocking collectives: 26.9 us -> none  [body(): lax.all_gather(step_blocks, 'seq', axis=0, tiled=True)]
    all_gather x1, blocking collectives: 21.6 us -> 26.3 us  [body(): lax.all_gather(tails, 'seq', axis=0, tiled=True)]
  transfers between devices with their start and end apart: 2 -> 17, of which waited for: 2 -> 3; matrix products, arithmetic and copies ran while one was open for 6% -> 10% of each run, Pallas kernels for 0% -> 0%
where the time goes in v1:
time: 443 us; the launch traced here: 442 us
  waiting for transfers between devices  219 us (49%)
  starting transfers between devices  63.7 us (14%)
  matrix products  55.3 us (12%)
  local copies, waits for them, and re-layouts  29.9 us (7%)
  blocking collectives  26.3 us (6%)
  other arithmetic  19.5 us (4%)
  between operations  17.4 us (4%)
  loops' own time  10.3 us (2%)
    all_gather x1, waiting for transfers between devices, body(): lax.all_gather(states, 'seq', axis=0, tiled=True)  149 us
    reduce_scatter x1, waiting for transfers between devices, body(): lax.psum_scatter(every_doc.astype(jnp.bfloat16), 'seq', scatter_dimension...  69.5 us
    ppermute x7, starting transfers between devices, ring_gather(): later.append(lax.ppermute(later[-1], axis, down))  41.9 us
    dot_general x1, matrix products, body(): jnp.einsum('ick,ckn->ikn', jnp.repeat(spans, HEAD_DIM, axis=2), lax.all_g...  38.9 us
    all_gather x1, blocking collectives, body(): lax.all_gather(tails, 'seq', axis=0, tiled=True)  26.3 us
    ppermute x8, starting transfers between devices, ring_gather(): earlier.append(lax.ppermute(earlier[-1], axis, up))  21.5 us
    another operation x1, loops' own time, body(): lax.map(one_doc, jnp.arange(DOCS, dtype=jnp.int32))  9.57 us
  transfers between devices with their start and end apart: 17, of which 3 were waited for; matrix products, arithmetic and copies ran while one was open for 10% of the time, Pallas kernels for 0%

profile of v1, /device:TPU:2, one launch (start us, length us, event | category | flops | bytes accessed | tf_op | source)
XLA Modules:
  0.0 441.8 jit_solution(11050842148515426330)
XLA Ops:
  7.2 3.4 collective-permute-start
  10.6 6.3 %collective-permute-start.8 = (bf16[1,256,40]{1,2,0:T(8,128)(2,1)}, bf16[1,256,40]{1,2,0:T(8,128)(2,1)S(1)}, u32[]{:S(2)}, u32[]{:S(2)}) collective-permute-start(bf16[1,256,40]{1,2,0:T(8,128)(2,1)} %bitcast.157), channel_id=1, source_target_pairs={{0,15},{1,0},{2,1},{3,2},{4,3},{5,4},{6,5},{7,6},{8,7},{9,8},{10,9... | collective-permute-start | bytes 61448 | tf_op jit(solution)/shard_map/ppermute | solution.py:24
  16.9 0.8 reduce-window.10
  17.8 1.2 dynamic_slice.66
  20.6 0.8 slice.76
  21.5 26.3 %all_gather.6 = bf16[16,3,2816]{2,1,0:T(4,128)(2,1)S(1)} all-gather(bf16[1,3,2816]{2,1,0:T(4,128)(2,1)S(1)} %slice.76), channel_id=1, replica_groups=mesh['dp'=32,'seq'=16] {'seq'}, dimensions={0}, use_global_device_ids=true | all-gather | bytes 287232 | tf_op jit(solution)/shard_map/all_gather | solution.py:64
  47.8 0.8 fusion.32
  48.6 1.1 slice_reduce_fusion.5
  49.8 1.9 collective-permute-start.1
  51.7 6.7 %multiply_convert_fusion.2 = bf16[1,256,2816]{2,1,0:T(8,128)(2,1)} fusion(bf16[256,2816]{1,0:T(8,128)(2,1)} %param.15, bf16[1,3,2816]{2,1,0:T(4,128)(2,1)S(1)} %copy.107, bf16[1,256,2816]{2,1,0:T(8,128)(2,1)} %bitcast.152, f32[2816]{0:T(1024)S(1)} %get-tuple-element.357, f32[256]{0:T(256)S(1)} %bitcast.172, f32[2816]{0:T(1024)S(1)} %get-tuple-element.358, ...), kind=kLoop, calls=%fused_computation.33 | loop fusion | flops 20905984 | bytes 4401664 | tf_op jit(solution)/shard_map/convert_element_type | solution.py:99
  58.4 4.5 %collective-permute-start.2 = (bf16[1,256,40]{1,2,0:T(8,128)(2,1)S(1)}, bf16[1,256,40]{1,2,0:T(8,128)(2,1)S(1)}, u32[]{:S(2)}, u32[]{:S(2)}) collective-permute-start(bf16[1,256,40]{1,2,0:T(8,128)(2,1)S(1)} %collective-permute-done.1), channel_id=1, source_target_pairs={{0,1},{1,2},{2,3},{3,4},{4,5},{5,6},{6,7},{7,8},{8,9},{9,10},{10,1... | collective-permute-start | bytes 61448 | tf_op jit(solution)/shard_map/ppermute | solution.py:22
  63.3 2.1 copy.73
  65.4 2.0 collective-permute-start.9
  67.5 3.9 collective-permute-start.3
  71.4 2.4 fusion.17
  74.4 4.6 %collective-permute-start.10 = (bf16[1,256,40]{1,2,0:T(8,128)(2,1)S(1)}, bf16[1,256,40]{1,2,0:T(8,128)(2,1)S(1)}, u32[]{:S(2)}, u32[]{:S(2)}) collective-permute-start(bf16[1,256,40]{1,2,0:T(8,128)(2,1)S(1)} %collective-permute-done.9), channel_id=1, source_target_pairs={{0,15},{1,0},{2,1},{3,2},{4,3},{5,4},{6,5},{7,6},{8,7},{9,8},{10,9... | collective-permute-start | bytes 61448 | tf_op jit(solution)/shard_map/ppermute | solution.py:24
  79.1 1.9 collective-permute-start.4
  81.2 7.2 %collective-permute-start.11 = (bf16[1,256,40]{1,2,0:T(8,128)(2,1)S(1)}, bf16[1,256,40]{1,2,0:T(8,128)(2,1)S(1)}, u32[]{:S(2)}, u32[]{:S(2)}) collective-permute-start(bf16[1,256,40]{1,2,0:T(8,128)(2,1)S(1)} %collective-permute-done.10), channel_id=1, source_target_pairs={{0,15},{1,0},{2,1},{3,2},{4,3},{5,4},{6,5},{7,6},{8,7},{9,8},{10,9... | collective-permute-start | bytes 61448 | tf_op jit(solution)/shard_map/ppermute | solution.py:24
  88.5 1.9 collective-permute-start.5
  90.4 7.2 %collective-permute-start.12 = (bf16[1,256,40]{1,2,0:T(8,128)(2,1)S(1)}, bf16[1,256,40]{1,2,0:T(8,128)(2,1)S(1)}, u32[]{:S(2)}, u32[]{:S(2)}) collective-permute-start(bf16[1,256,40]{1,2,0:T(8,128)(2,1)S(1)} %collective-permute-done.11), channel_id=1, source_target_pairs={{0,15},{1,0},{2,1},{3,2},{4,3},{5,4},{6,5},{7,6},{8,7},{9,8},{10,9... | collective-permute-start | bytes 61448 | tf_op jit(solution)/shard_map/ppermute | solution.py:24
  97.7 1.9 collective-permute-start.6
  102.2 7.2 %collective-permute-start.13 = (bf16[1,256,40]{1,2,0:T(8,128)(2,1)S(1)}, bf16[1,256,40]{1,2,0:T(8,128)(2,1)S(1)}, u32[]{:S(2)}, u32[]{:S(2)}) collective-permute-start(bf16[1,256,40]{1,2,0:T(8,128)(2,1)S(1)} %collective-permute-done.12), channel_id=1, source_target_pairs={{0,15},{1,0},{2,1},{3,2},{4,3},{5,4},{6,5},{7,6},{8,7},{9,8},{10,9... | collective-permute-start | bytes 61448 | tf_op jit(solution)/shard_map/ppermute | solution.py:24
  109.4 1.9 collective-permute-start.7
  112.2 7.2 %collective-permute-start.14 = (bf16[1,256,40]{1,2,0:T(8,128)(2,1)S(1)}, bf16[1,256,40]{1,2,0:T(8,128)(2,1)S(1)}, u32[]{:S(2)}, u32[]{:S(2)}) collective-permute-start(bf16[1,256,40]{1,2,0:T(8,128)(2,1)S(1)} %collective-permute-done.13), channel_id=1, source_target_pairs={{0,15},{1,0},{2,1},{3,2},{4,3},{5,4},{6,5},{7,6},{8,7},{9,8},{10,9... | collective-permute-start | bytes 61448 | tf_op jit(solution)/shard_map/ppermute | solution.py:24
  119.6 1.3 collective-permute-done.14
  121.9 0.8 fusion.42
  123.7 1.7 broadcast_in_dim.184
  125.4 3.2 copy.78
  128.6 3.5 fusion.25
  132.4 1.4 copy.74
  133.8 0.8 slice.87
  135.7 148.5 %all-gather.3.cloned.1.call-done = f32[40960,128]{1,0:T(8,128)} async-done(((f32[2560,128]{1,0:T(8,128)}), f32[40960,128]{1,0:T(8,128)}) %all-gather.3.cloned.1.call-update) | async-done | bytes 20971536 | tf_op jit(solution)/shard_map/all_gather | solution.py:123
  284.3 38.9 %fusion.6 = f32[2560,1,128]{2,1,0:T(1,128)S(1)} fusion(f32[16,2560,1]{0,2,1:T(1,128)S(1)} %bitcast.150, f32[16,2560,128]{2,1,0:T(8,128)} %bitcast.146), kind=kOutput, calls=%fused_computation.15 | convolution fusion | flops 62914560 | bytes 22446080 | tf_op jit(solution)/shard_map/ick,ckn->ikn/dot_general | solution.py:120
  323.2 20.1 %while.17 = (s32[]{:T(128)}, bf16[3,2560,128]{2,1,0:T(8,128)(2,1)}, s32[3]{0:T(128)S(1)}, s32[3]{0:T(128)S(1)}, s32[1]{0:T(128)}, /*index=5*/bf16[1,256,2560]{1,...) while((s32[]{:T(128)}, bf16[3,2560,128]{2,1,0:T(8,128)(2,1)}, ...), condition=%wide.region_13.14_spmd, body=%wide.region_10.13_spmd.sunk | while | flops 170742112 | bytes 7442075 | solution.py:195
  327.6 4.0 conditional.2
  328.6 1.7 fusion.1
  331.6 0.9 constant_dynamic-update-slice_fusion.34
  337.0 0.9 constant_dynamic-update-slice_fusion.34
  342.4 0.9 constant_dynamic-update-slice_fusion.34
  343.6 1.1 fusion.36
  344.8 1.7 broadcast_in_dim.192
  346.5 3.2 copy.79
  349.7 4.8 %fusion.8 = f32[40,64,256]{2,1,0:T(8,128)} fusion(bf16[256,40,64]{0,2,1:T(8,128)(2,1)} %bitcast.28, f32[40,256]{1,0:T(8,128)S(1)} %bitcast.153, f32[256,256]{1,0:T(8,128)S(1)} %fusion.36, pred[256,256]{1,0:T(8,128)(4,1)S(1)} %fusion.34), kind=kOutput, calls=%fused_computation.18 | convolution fusion | flops 346030080 | bytes 4300800 | tf_op jit(solution)/shard_map/while/body/eval_jaxpr/hts,shp->thp/dot_general | solution.py:137
  354.5 3.4 copy.80
  357.9 4.6 %multiply_reduce_fusion = (f32[256]{0:T(256)S(1)}, f32[256,2560]{1,0:T(8,128)S(1)}) fusion(bf16[256,2560]{1,0:T(8,128)(2,1)S(1)} %copy-done.5, f32[2560]{0:T(1024)S(1)} %mul.239, bf16[1,256,2816]{2,1,0:T(8,128)(2,1)} %multiply_convert_fusion.2, f32[256,2560]{1,0:T(8,128)} %copy.80, f32[256,2560]{1,0:T(8,128)} %copy.79, f32[2560,128]{1,0:T(8,128)S(1)} %bitcast.145), kind=kOutput, calls=%fused_computation.40 | convolution fusion | flops 176619264 | bytes 11873280 | tf_op jit(solution)/shard_map/while/body/eval_jaxpr/dot_general | solution.py:143
  362.5 1.3 multiply_convert_fusion.3
  363.8 69.5 %reduce-scatter.2.cloned.1.call-done = bf16[160,3,128]{2,0,1:T(8,128)(2,1)} async-done(((bf16[2560,3,128]{2,0,1:T(8,128)(2,1)}), bf16[160,3,128]{2,0,1:T(8,128)(2,1)}) %reduce-scatter.2.cloned.1.call-update) | async-done | bytes 122896 | tf_op jit(solution)/shard_map/reduce_scatter | solution.py:196
  433.3 1.6 convert_bitcast_fusion.2
  (122 shorter events, 12.9 us)
Async XLA Ops:
  7.2 277.0 %all-gather.3.cloned.1.call-start = ((), (), s32[]{:S(2)}) async-start(), calls=%async_computation.2 | async-start | bytes 22282240 | tf_op jit(solution)/shard_map/all_gather | solution.py:123
  7.2 42.5 %collective-permute-start = (bf16[1,256,40]{1,2,0:T(8,128)(2,1)}, bf16[1,256,40]{1,2,0:T(8,128)(2,1)S(1)}, u32[]{:S(2)}, u32[]{:S(2)}) collective-permute-start(bf16[1,256,40]{1,2,0:T(8,128)(2,1)} %bitcast.156), channel_id=1, source_target_pairs={{0,1},{1,2},{2,3},{3,4},{4,5},{5,6},{6,7},{7,8},{8,9},{9,10},{10,1... | collective-permute-start | bytes 61448 | tf_op jit(solution)/shard_map/ppermute | solution.py:22
  10.6 54.8 %collective-permute-start.8 = (bf16[1,256,40]{1,2,0:T(8,128)(2,1)}, bf16[1,256,40]{1,2,0:T(8,128)(2,1)S(1)}, u32[]{:S(2)}, u32[]{:S(2)}) collective-permute-start(bf16[1,256,40]{1,2,0:T(8,128)(2,1)} %bitcast.157), channel_id=1, source_target_pairs={{0,15},{1,0},{2,1},{3,2},{4,3},{5,4},{6,5},{7,6},{8,7},{9,8},{10,9... | collective-permute-start | bytes 61448 | tf_op jit(solution)/shard_map/ppermute | solution.py:24
  21.4 37.0 %copy-start.6 = (f32[40]{0:T(128)S(1)}, f32[40]{0:T(128)}, u32[]{:S(2)}) copy-start(f32[40]{0:T(128)} %param.23) | copy-start | bytes 484
  21.4 41.6 %copy-start = (bf16[256,40]{0,1:T(8,128)(2,1)S(1)}, bf16[256,40]{0,1:T(8,128)(2,1)}, u32[]{:S(2)}) copy-start(bf16[256,40]{0,1:T(8,128)(2,1)} %param.17) | copy-start | bytes 61444
  21.4 41.6 %copy-start.3 = (f32[40]{0:T(128)S(1)}, f32[40]{0:T(128)}, u32[]{:S(2)}) copy-start(f32[40]{0:T(128)} %param.22) | copy-start | bytes 484
  49.8 8.7 %collective-permute-start.1 = (bf16[1,256,40]{1,2,0:T(8,128)(2,1)S(1)}, bf16[1,256,40]{1,2,0:T(8,128)(2,1)S(1)}, u32[]{:S(2)}, u32[]{:S(2)}) collective-permute-start(bf16[1,256,40]{1,2,0:T(8,128)(2,1)S(1)} %collective-permute-done), channel_id=1, source_target_pairs={{0,1},{1,2},{2,3},{3,4},{4,5},{5,6},{6,7},{7,8},{8,9},{9,10},{10,1... | collective-permute-start | bytes 61448 | tf_op jit(solution)/shard_map/ppermute | solution.py:22
  58.4 9.0 %collective-permute-start.2 = (bf16[1,256,40]{1,2,0:T(8,128)(2,1)S(1)}, bf16[1,256,40]{1,2,0:T(8,128)(2,1)S(1)}, u32[]{:S(2)}, u32[]{:S(2)}) collective-permute-start(bf16[1,256,40]{1,2,0:T(8,128)(2,1)S(1)} %collective-permute-done.1), channel_id=1, source_target_pairs={{0,1},{1,2},{2,3},{3,4},{4,5},{5,6},{6,7},{7,8},{8,9},{9,10},{10,1... | collective-permute-start | bytes 61448 | tf_op jit(solution)/shard_map/ppermute | solution.py:22
  65.4 56.2 %copy-start.2 = (s32[16]{0:T(128)S(1)}, s32[16]{0:T(128)}, u32[]{:S(2)}) copy-start(s32[16]{0:T(128)} %param.19) | copy-start | bytes 196
  65.4 9.0 %collective-permute-start.9 = (bf16[1,256,40]{1,2,0:T(8,128)(2,1)S(1)}, bf16[1,256,40]{1,2,0:T(8,128)(2,1)S(1)}, u32[]{:S(2)}, u32[]{:S(2)}) collective-permute-start(bf16[1,256,40]{1,2,0:T(8,128)(2,1)S(1)} %collective-permute-done.8), channel_id=1, source_target_pairs={{0,15},{1,0},{2,1},{3,2},{4,3},{5,4},{6,5},{7,6},{8,7},{9,8},{10,9... | collective-permute-start | bytes 61448 | tf_op jit(solution)/shard_map/ppermute | solution.py:24
  67.5 11.6 %collective-permute-start.3 = (bf16[1,256,40]{1,2,0:T(8,128)(2,1)S(1)}, bf16[1,256,40]{1,2,0:T(8,128)(2,1)S(1)}, u32[]{:S(2)}, u32[]{:S(2)}) collective-permute-start(bf16[1,256,40]{1,2,0:T(8,128)(2,1)S(1)} %collective-permute-done.2), channel_id=1, source_target_pairs={{0,1},{1,2},{2,3},{3,4},{4,5},{5,6},{6,7},{7,8},{8,9},{9,10},{10,1... | collective-permute-start | bytes 61448 | tf_op jit(solution)/shard_map/ppermute | solution.py:22
  74.4 6.8 %collective-permute-start.10 = (bf16[1,256,40]{1,2,0:T(8,128)(2,1)S(1)}, bf16[1,256,40]{1,2,0:T(8,128)(2,1)S(1)}, u32[]{:S(2)}, u32[]{:S(2)}) collective-permute-start(bf16[1,256,40]{1,2,0:T(8,128)(2,1)S(1)} %collective-permute-done.9), channel_id=1, source_target_pairs={{0,15},{1,0},{2,1},{3,2},{4,3},{5,4},{6,5},{7,6},{8,7},{9,8},{10,9... | collective-permute-start | bytes 61448 | tf_op jit(solution)/shard_map/ppermute | solution.py:24
  79.1 9.4 %collective-permute-start.4 = (bf16[1,256,40]{1,2,0:T(8,128)(2,1)S(1)}, bf16[1,256,40]{1,2,0:T(8,128)(2,1)S(1)}, u32[]{:S(2)}, u32[]{:S(2)}) collective-permute-start(bf16[1,256,40]{1,2,0:T(8,128)(2,1)S(1)} %collective-permute-done.3), channel_id=1, source_target_pairs={{0,1},{1,2},{2,3},{3,4},{4,5},{5,6},{6,7},{7,8},{8,9},{9,10},{10,1... | collective-permute-start | bytes 61448 | tf_op jit(solution)/shard_map/ppermute | solution.py:22
  81.2 9.2 %collective-permute-start.11 = (bf16[1,256,40]{1,2,0:T(8,128)(2,1)S(1)}, bf16[1,256,40]{1,2,0:T(8,128)(2,1)S(1)}, u32[]{:S(2)}, u32[]{:S(2)}) collective-permute-start(bf16[1,256,40]{1,2,0:T(8,128)(2,1)S(1)} %collective-permute-done.10), channel_id=1, source_target_pairs={{0,15},{1,0},{2,1},{3,2},{4,3},{5,4},{6,5},{7,6},{8,7},{9,8},{10,9... | collective-permute-start | bytes 61448 | tf_op jit(solution)/shard_map/ppermute | solution.py:24
  88.5 9.2 %collective-permute-start.5 = (bf16[1,256,40]{1,2,0:T(8,128)(2,1)S(1)}, bf16[1,256,40]{1,2,0:T(8,128)(2,1)S(1)}, u32[]{:S(2)}, u32[]{:S(2)}) collective-permute-start(bf16[1,256,40]{1,2,0:T(8,128)(2,1)S(1)} %collective-permute-done.4), channel_id=1, source_target_pairs={{0,1},{1,2},{2,3},{3,4},{4,5},{5,6},{6,7},{7,8},{8,9},{9,10},{10,1... | collective-permute-start | bytes 61448 | tf_op jit(solution)/shard_map/ppermute | solution.py:22
  90.4 11.7 %collective-permute-start.12 = (bf16[1,256,40]{1,2,0:T(8,128)(2,1)S(1)}, bf16[1,256,40]{1,2,0:T(8,128)(2,1)S(1)}, u32[]{:S(2)}, u32[]{:S(2)}) collective-permute-start(bf16[1,256,40]{1,2,0:T(8,128)(2,1)S(1)} %collective-permute-done.11), channel_id=1, source_target_pairs={{0,15},{1,0},{2,1},{3,2},{4,3},{5,4},{6,5},{7,6},{8,7},{9,8},{10,9... | collective-permute-start | bytes 61448 | tf_op jit(solution)/shard_map/ppermute | solution.py:24
  97.7 11.7 %collective-permute-start.6 = (bf16[1,256,40]{1,2,0:T(8,128)(2,1)S(1)}, bf16[1,256,40]{1,2,0:T(8,128)(2,1)S(1)}, u32[]{:S(2)}, u32[]{:S(2)}) collective-permute-start(bf16[1,256,40]{1,2,0:T(8,128)(2,1)S(1)} %collective-permute-done.5), channel_id=1, source_target_pairs={{0,1},{1,2},{2,3},{3,4},{4,5},{5,6},{6,7},{7,8},{8,9},{9,10},{10,1... | collective-permute-start | bytes 61448 | tf_op jit(solution)/shard_map/ppermute | solution.py:22
  102.2 10.0 %collective-permute-start.13 = (bf16[1,256,40]{1,2,0:T(8,128)(2,1)S(1)}, bf16[1,256,40]{1,2,0:T(8,128)(2,1)S(1)}, u32[]{:S(2)}, u32[]{:S(2)}) collective-permute-start(bf16[1,256,40]{1,2,0:T(8,128)(2,1)S(1)} %collective-permute-done.12), channel_id=1, source_target_pairs={{0,15},{1,0},{2,1},{3,2},{4,3},{5,4},{6,5},{7,6},{8,7},{9,8},{10,9... | collective-permute-start | bytes 61448 | tf_op jit(solution)/shard_map/ppermute | solution.py:24
  109.4 10.0 %collective-permute-start.7 = (bf16[1,256,40]{1,2,0:T(8,128)(2,1)S(1)}, bf16[1,256,40]{1,2,0:T(8,128)(2,1)S(1)}, u32[]{:S(2)}, u32[]{:S(2)}) collective-permute-start(bf16[1,256,40]{1,2,0:T(8,128)(2,1)S(1)} %collective-permute-done.6), channel_id=1, source_target_pairs={{0,1},{1,2},{2,3},{3,4},{4,5},{5,6},{6,7},{7,8},{8,9},{9,10},{10,1... | collective-permute-start | bytes 61448 | tf_op jit(solution)/shard_map/ppermute | solution.py:22
  112.2 8.7 %collective-permute-start.14 = (bf16[1,256,40]{1,2,0:T(8,128)(2,1)S(1)}, bf16[1,256,40]{1,2,0:T(8,128)(2,1)S(1)}, u32[]{:S(2)}, u32[]{:S(2)}) collective-permute-start(bf16[1,256,40]{1,2,0:T(8,128)(2,1)S(1)} %collective-permute-done.13), channel_id=1, source_target_pairs={{0,15},{1,0},{2,1},{3,2},{4,3},{5,4},{6,5},{7,6},{8,7},{9,8},{10,9... | collective-permute-start | bytes 61448 | tf_op jit(solution)/shard_map/ppermute | solution.py:24
  132.2 301.2 %reduce-scatter.2.cloned.1.call-start = ((), (), s32[]{:S(2)}) async-start(), calls=%async_computation.1 | async-start | bytes 2088960 | tf_op jit(solution)/shard_map/reduce_scatter | solution.py:196
  323.2 20.2 %copy-start.4 = (f32[40]{0:T(128)S(1)}, f32[40]{0:T(128)}, u32[]{:S(2)}) copy-start(f32[40]{0:T(128)} %param.24) | copy-start | bytes 484
  354.5 3.4 copy-start.5
  357.9 4.6 %copy-start.1 = (f32[2560]{0:T(1024)S(1)}, f32[2560]{0:T(1024)}, u32[]{:S(2)}) copy-start(f32[2560]{0:T(1024)} %param.25) | copy-start | bytes 30724
Sparse Core Ops, SparseCore 0:
  132.3 151.8 all-gather.2
  343.5 89.8 reduce-scatter.1
